TPU v7x, 128 devices: a whole 4x4x4 slice. The times are simulated.
128 devices in a mesh: req: 8 (over z, core), mp: 16 (over x, y).
Axes of the slice: x: 4, y: 4, z: 4, core: 2. Of those that a mesh axis runs over, the one named last changes fastest.
Arguments:
- states: bfloat16 [8, 32, 16, 5120], P('req', None, 'mp'), may hold values from -6 to 6
- lengths: int32 [8, 4], replicated, may hold values from 1 to 509, as said below
- request_adapters: int32 [8, 4], replicated, may hold values from 0 to 7
- attention_norm_gain: float32 [5120], replicated, may hold values from 0.1 to 1.9
- query_weight: bfloat16 [5120, 4096], P(None, 'mp')
- key_weight: bfloat16 [5120, 1024], P(None, 'mp')
- value_weight: bfloat16 [5120, 1024], P(None, 'mp'), may hold values from -0.078125 to 0.078125
- output_weight: bfloat16 [4096, 5120], P('mp'), may hold values from -0.09375 to 0.09375
- adapter_down_attention: bfloat16 [5120, 384], replicated, may hold values from -0.078125 to 0.078125
- adapter_up_query: bfloat16 [128, 4096], P(None, 'mp'), may hold values from -0.5 to 0.5
- adapter_up_key_value: bfloat16 [2, 128, 1024], P(None, None, 'mp'), may hold values from -0.5 to 0.5
- adapter_down_output: bfloat16 [4096, 128], P('mp'), may hold values from -0.09375 to 0.09375
- adapter_up_output: bfloat16 [128, 5120], replicated, may hold values from -0.875 to 0.875
- feed_norm_gain: float32 [5120], replicated, may hold values from 0.1 to 1.9
- gate_up_weight: bfloat16 [2, 5120, 10240], P(None, 'req', 'mp'), may hold values from -0.078125 to 0.078125
- down_weight: bfloat16 [5120, 10240], P('req', 'mp'), may hold values from -0.0625 to 0.0625
- adapter_down_gate_up: bfloat16 [5120, 256], replicated, may hold values from -0.078125 to 0.078125
- adapter_up_gate_up: bfloat16 [2, 128, 10240], P(None, None, 'mp'), may hold values from -0.5 to 0.5
- adapter_down_feed: bfloat16 [10240, 128], P('mp'), may hold values from -0.0625 to 0.0625
- adapter_up_feed: bfloat16 [128, 5120], replicated, may hold values from -0.875 to 0.875
Outputs:
- layer_out: bfloat16 [8, 32, 16, 5120], P('req', None, 'mp')
Inputs may be any that keep to these rules, and one draw needn't show every extreme that they name: `lengths`: each request has at least one token; each row sums to at most 512, some row to exactly 512, and all rows together to exactly 2048; some request is 509 tokens long.
All inputs are finite; a program needn't handle non-finite values.
Results may differ from a plain program's by a relative error of at most 0.03.
Values may be sent and summed in bfloat16 or wider, within the bound.
No kernel may reach another device: no remote copies, remote signals or barrier semaphores. Data moves between devices by JAX's collectives and lax.ppermute only.
A program may use at most 128 MiB of HBM per device.

v0:
```python
import jax
import jax.numpy as jnp
from jax import lax
from jax.sharding import PartitionSpec as P

HEAD_SIZE = 128
ADAPTER_RANK = 16
WINDOW = 128
SINK = 4
EPSILON = 1e-05
ROPE_THETA = 1000000.0


def from_partner(shard, axis, stride):
    return lax.ppermute(shard, axis, [(i, i ^ 1 << stride) for i in range(lax.axis_size(axis))])


def slot_info(length_rows, adapter_rows, slot_ids):
    request_ends = jnp.cumsum(length_rows, axis=1, dtype=jnp.int32)
    starts = request_ends - length_rows
    count_req = length_rows.shape[1]
    request = jnp.sum(
        (slot_ids[:, None] >= request_ends).astype(jnp.int32), axis=1, dtype=jnp.int32
    )
    living = request < count_req
    matches = request[:, None] == jnp.arange(count_req, dtype=jnp.int32)[None, :]
    opening = jnp.sum(jnp.where(matches, starts, 0), axis=1, dtype=jnp.int32)
    position = jnp.where(living, slot_ids - opening, 0)
    segment = jnp.where(living, request, count_req + slot_ids)
    chosen = jnp.sum(jnp.where(matches, adapter_rows, 0), axis=1, dtype=jnp.int32)
    adapter_slot = jnp.where(living, chosen, -1)
    return (living, position, segment, adapter_slot)


def normalize(input_tokens, gain_vec):
    values = input_tokens.astype(jnp.float32)
    factor = lax.rsqrt(jnp.mean(values * values, axis=-1, keepdims=True) + EPSILON)
    return (values * factor * gain_vec).astype(jnp.bfloat16)


def adapter_select_mask(adapter_slot, adapter_column_count, adapter_rank_size):
    token_owner_request = jnp.arange(adapter_column_count, dtype=jnp.int32) // adapter_rank_size
    return (adapter_slot[:, None] == token_owner_request[None, :]).astype(jnp.float32)


def rotate(vectors, position):
    half_dim = vectors.shape[-1] // 2
    inverse = ROPE_THETA ** (-(jnp.arange(half_dim, dtype=jnp.float32) * (2.0 / vectors.shape[-1])))
    angles = position.astype(jnp.float32)[:, None] * inverse[None, :]
    cosine = jnp.cos(angles)[:, None, :]
    sine_part = jnp.sin(angles)[:, None, :]
    lower_half = vectors[..., :half_dim]
    upper_half = vectors[..., half_dim:]
    return jnp.concatenate(
        [
            lower_half * cosine - upper_half * sine_part,
            upper_half * cosine + lower_half * sine_part,
        ],
        axis=-1,
    )


def attend(queries, key_rows, value_rows, position, segment):
    key_heads = key_rows.shape[1]
    group_size = queries.shape[1] // key_heads
    token_count = queries.shape[0]
    grouped_queries = queries.reshape(token_count, key_heads, group_size, queries.shape[2])
    scores = jnp.einsum(
        "qkgd,skd->kgqs", grouped_queries, key_rows, preferred_element_type=jnp.float32
    ) * queries.shape[2] ** (-0.5)
    allowed = (segment[:, None] == segment[None, :]) & (position[None, :] <= position[:, None])
    allowed = allowed & (
        (position[:, None] - position[None, :] < WINDOW) | (position[None, :] < SINK)
    )
    scores = jnp.where(allowed[None, None], scores, -jnp.inf)
    highest = jnp.max(scores, axis=-1, keepdims=True)
    weights_raw = jnp.exp(scores - highest)
    weights = (weights_raw / jnp.sum(weights_raw, axis=-1, keepdims=True)).astype(jnp.bfloat16)
    blended = jnp.einsum("kgqs,skd->qkgd", weights, value_rows, preferred_element_type=jnp.float32)
    return blended.reshape(token_count, -1).astype(jnp.bfloat16)


def spread_rows(first_part, second_part):
    return (
        lax.all_gather(first_part, "mp", axis=0, tiled=True),
        lax.all_gather(second_part, "mp", axis=0, tiled=True),
    )


def sum_rows(term_fn, row_count):
    return lax.psum_scatter(
        term_fn(jnp.int32(0), lax.axis_size("mp") * row_count).astype(jnp.bfloat16),
        "mp",
        scatter_dimension=0,
        tiled=True,
    ).astype(jnp.float32)


def feed_forward(
    residual_stream,
    adapter_indicator,
    feed_norm_gain,
    adapter_down_gate_up,
    adapter_up_gate_up,
    gate_up_full,
    down_full,
    adapter_down_feed,
    adapter_up_feed,
):
    adapter_column_count = adapter_indicator.shape[1]
    model_width = residual_stream.shape[1]
    feed_input = normalize(residual_stream, feed_norm_gain)
    gate_terms = (
        jnp.dot(feed_input, adapter_down_gate_up, preferred_element_type=jnp.float32)
        * jnp.tile(adapter_indicator, (1, 2))
    ).astype(jnp.bfloat16)
    mlp_all, gate_adapter_ranks = spread_rows(feed_input, gate_terms)
    gate_activation = jnp.dot(
        mlp_all, gate_up_full[0], preferred_element_type=jnp.float32
    ) + jnp.dot(
        gate_adapter_ranks[:, :adapter_column_count],
        adapter_up_gate_up[0],
        preferred_element_type=jnp.float32,
    )
    up_projected = jnp.dot(mlp_all, gate_up_full[1], preferred_element_type=jnp.float32) + jnp.dot(
        gate_adapter_ranks[:, adapter_column_count:],
        adapter_up_gate_up[1],
        preferred_element_type=jnp.float32,
    )
    hidden_activation = (jax.nn.silu(gate_activation) * up_projected).astype(jnp.bfloat16)

    def down_term(first_row, row_count):
        projected_rows = lax.dot_general(
            hidden_activation,
            down_full,
            (((1,), (1,)), ((), ())),
            preferred_element_type=jnp.float32,
        )
        return jnp.concatenate(
            [
                projected_rows,
                jnp.dot(hidden_activation, adapter_down_feed, preferred_element_type=jnp.float32),
            ],
            axis=1,
        )

    summed = sum_rows(down_term, residual_stream.shape[0])
    down_adapter_ranks = (summed[:, model_width:] * adapter_indicator).astype(jnp.bfloat16)
    return (
        residual_stream.astype(jnp.float32)
        + summed[:, :model_width]
        + jnp.dot(down_adapter_ranks, adapter_up_feed, preferred_element_type=jnp.float32)
    )


def shards(
    states,
    lengths,
    request_adapters,
    attention_norm_gain,
    query_weight,
    key_weight,
    value_weight,
    output_weight,
    adapter_down_attention,
    adapter_up_query,
    adapter_up_key_value,
    adapter_down_output,
    adapter_up_output,
    feed_norm_gain,
    gate_up_weight,
    down_weight,
    adapter_down_gate_up,
    adapter_up_gate_up,
    adapter_down_feed,
    adapter_up_feed,
):
    mp_count = lax.axis_size("mp")
    group_index = lax.axis_index("req")
    mp_index = lax.axis_index("mp")
    slot_dev = states.shape[1]
    model_width = states.shape[3]
    adapter_column_count = adapter_up_output.shape[0]
    total_rows = slot_dev * mp_count
    gate_up_full, down_full = (
        lax.all_gather(gate_up_weight, "req", axis=1, tiled=True),
        lax.all_gather(down_weight, "req", axis=0, tiled=True),
    )
    local_rows = states.reshape(slot_dev, model_width)
    own_lengths = lax.dynamic_index_in_dim(lengths, group_index, 0, keepdims=False)
    own_adapters = lax.dynamic_index_in_dim(request_adapters, group_index, 0, keepdims=False)
    request_count = own_lengths.shape[0]
    local_slots = jnp.arange(slot_dev, dtype=jnp.int32) * mp_count + mp_index
    living, unused_pos, unused_seg, adapter_within = slot_info(
        jnp.broadcast_to(own_lengths[None, :], (slot_dev, request_count)),
        jnp.broadcast_to(own_adapters[None, :], (slot_dev, request_count)),
        local_slots,
    )
    indicator_within = adapter_select_mask(adapter_within, adapter_column_count, ADAPTER_RANK)
    normed_rows = normalize(local_rows, attention_norm_gain)
    down_adapter_terms = (
        jnp.dot(normed_rows, adapter_down_attention, preferred_element_type=jnp.float32)
        * jnp.tile(indicator_within, (1, 3))
    ).astype(jnp.bfloat16)
    normed_all, adapter_terms_all = spread_rows(normed_rows, down_adapter_terms)
    gathered = jnp.arange(total_rows, dtype=jnp.int32)
    gathered_slots = gathered % slot_dev * mp_count + gathered // slot_dev
    ignored, position_all, segment_all, unused = slot_info(
        jnp.broadcast_to(own_lengths[None, :], (total_rows, request_count)),
        jnp.broadcast_to(own_adapters[None, :], (total_rows, request_count)),
        gathered_slots,
    )
    query_projected = jnp.dot(
        normed_all, query_weight, preferred_element_type=jnp.float32
    ) + jnp.dot(
        adapter_terms_all[:, :adapter_column_count],
        adapter_up_query,
        preferred_element_type=jnp.float32,
    )
    key_projected = jnp.dot(normed_all, key_weight, preferred_element_type=jnp.float32) + jnp.dot(
        adapter_terms_all[:, adapter_column_count : 2 * adapter_column_count],
        adapter_up_key_value[0],
        preferred_element_type=jnp.float32,
    )
    value_projected = jnp.dot(
        normed_all, value_weight, preferred_element_type=jnp.float32
    ) + jnp.dot(
        adapter_terms_all[:, 2 * adapter_column_count :],
        adapter_up_key_value[1],
        preferred_element_type=jnp.float32,
    )
    kv_pair = jnp.stack([key_projected, value_projected])
    partner = from_partner(kv_pair.astype(jnp.bfloat16), "mp", 0).astype(kv_pair.dtype)
    parity = mp_index % 2
    joined = jnp.where(
        parity == 0,
        jnp.concatenate([kv_pair, partner], axis=2),
        jnp.concatenate([partner, kv_pair], axis=2),
    )
    key_projected = joined[0]
    value_projected = joined[1]
    queries = rotate(query_projected.reshape(total_rows, -1, HEAD_SIZE), position_all).astype(
        jnp.bfloat16
    )
    key_rows = rotate(key_projected.reshape(total_rows, -1, HEAD_SIZE), position_all).astype(
        jnp.bfloat16
    )
    value_rows = value_projected.reshape(total_rows, -1, HEAD_SIZE).astype(jnp.bfloat16)
    attention_output = attend(queries, key_rows, value_rows, position_all, segment_all)

    def out_term(first_row, row_count):
        return jnp.concatenate(
            [
                jnp.dot(attention_output, output_weight, preferred_element_type=jnp.float32),
                jnp.dot(attention_output, adapter_down_output, preferred_element_type=jnp.float32),
            ],
            axis=1,
        )

    summed = sum_rows(out_term, slot_dev)
    output_adapter_ranks = (summed[:, model_width:] * indicator_within).astype(jnp.bfloat16)
    residual_stream = (
        local_rows.astype(jnp.float32)
        + summed[:, :model_width]
        + jnp.dot(output_adapter_ranks, adapter_up_output, preferred_element_type=jnp.float32)
    ).astype(jnp.bfloat16)
    layer_result = feed_forward(
        residual_stream,
        indicator_within,
        feed_norm_gain,
        adapter_down_gate_up,
        adapter_up_gate_up,
        gate_up_full,
        down_full,
        adapter_down_feed,
        adapter_up_feed,
    )
    finished = jnp.where(living[:, None], layer_result, jnp.zeros_like(layer_result)).astype(
        jnp.bfloat16
    )
    return finished.reshape(1, slot_dev, 1, model_width)


def solution(mesh):
    placed = (
        P("req", None, "mp", None),
        P(),
        P(),
        P(),
        P(None, "mp"),
        P(None, "mp"),
        P(None, "mp"),
        P("mp", None),
        P(),
        P(None, "mp"),
        P(None, None, "mp"),
        P("mp", None),
        P(),
        P(),
        P(None, "req", "mp"),
        P("req", "mp"),
        P(),
        P(None, None, "mp"),
        P("mp", None),
        P(),
    )
    return jax.shard_map(
        shards, mesh=mesh, in_specs=placed, out_specs=P("req", None, "mp", None), check_vma=False
    )
```

profile of v0, /device:TPU:0, one launch (start us, length us, event | category | flops | bytes accessed | tf_op | source)
XLA Modules:
  0.0 374.3 jit_solution(9356517427873892993)
XLA Ops:
  7.4 1.3 fusion.17
  8.7 1.9 fusion.19
  10.6 0.9 dynamic-slice_reduce_fusion
  12.0 0.3 copy-done.21
  12.3 2.9 fusion.12
  15.2 25.0 %all_gather.19 = bf16[512,384]{1,0:T(8,128)(2,1)S(1)} all-gather(bf16[32,384]{1,0:T(8,128)(2,1)S(1)} %fusion.12), channel_id=1, replica_groups=mesh['req'=8,'mp'=16] {'mp'}, dimensions={0}, use_global_device_ids=true | all-gather | bytes 417792 | tf_op jit(solution)/shard_map/all_gather | solution.py:86
  40.4 1.2 fusion.16
  41.6 1.8 multiply_cosine_fusion
  43.4 26.8 %all-gather.5.cloned.1.call-done = bf16[512,5120]{1,0:T(8,128)(2,1)} async-done(((bf16[32,5120]{1,0:T(8,128)(2,1)}), bf16[512,5120]{1,0:T(8,128)(2,1)}) %all-gather.5.cloned.1.call-update) | async-done | bytes 5242896 | tf_op jit(solution)/shard_map/all_gather | solution.py:85
  70.2 4.5 %fusion.76 = f32[512,64]{0,1:T(8,128)S(1)} fusion(bf16[512,5120]{1,0:T(8,128)(2,1)} %all-gather.5.cloned.1.call-done, bf16[5120,64]{0,1:T(8,128)(2,1)} %param.26), kind=kOutput, calls=%fused_computation.140 | convolution fusion | flops 335544320 | bytes 6029312 | tf_op jit(solution)/shard_map/dot_general | solution.py:225
  74.9 1.7 fusion.75
  76.8 0.7 maximum_convert_fusion
  77.5 1.4 collective-permute-start
  78.9 1.6 fusion.77
  80.5 0.3 convolution_add_fusion.4
  80.8 0.8 fusion.73
  81.6 1.1 copy.44
  82.7 1.9 copy.45
  84.7 1.4 subtract_convert_fusion
  86.2 0.6 fusion.45
  86.8 0.6 fusion.74
  87.4 0.3 fusion.7
  87.7 0.5 convolution_convert_fusion.2
  88.3 1.6 convolution_convert_fusion
  89.8 0.3 convolution_convert_fusion.4
  90.1 2.7 pad_maximum_fusion
  92.9 0.5 all-gather.9.cloned.1.call-update
  93.7 78.0 %reduce-scatter.3.cloned.1.call-done = bf16[32,5248]{1,0:T(8,128)(2,1)} async-done(((bf16[512,5248]{1,0:T(8,128)(2,1)}), bf16[32,5248]{1,0:T(8,128)(2,1)}) %reduce-scatter.3.cloned.1.call-update) | async-done | bytes 335888 | tf_op jit(solution)/shard_map/reduce_scatter | solution.py:91
  171.7 1.0 convert_element_type.118
  172.8 0.5 multiply_reduce_fusion
  173.3 0.9 multiply_convert_fusion
  174.2 0.5 all-gather.11.cloned.1.call-update
  174.8 2.4 fusion.13
  177.2 23.4 %all_gather.22 = bf16[512,256]{1,0:T(8,128)(2,1)S(1)} all-gather(bf16[32,256]{1,0:T(8,128)(2,1)S(1)} %fusion.13), channel_id=1, replica_groups=mesh['req'=8,'mp'=16] {'mp'}, dimensions={0}, use_global_device_ids=true | all-gather | bytes 278528 | tf_op jit(solution)/shard_map/all_gather | solution.py:86
  200.7 29.8 %all-gather.7.cloned.1.call-done = bf16[512,5120]{1,0:T(8,128)(2,1)} async-done(((bf16[32,5120]{1,0:T(8,128)(2,1)}), bf16[512,5120]{1,0:T(8,128)(2,1)}) %all-gather.7.cloned.1.call-update) | async-done | bytes 5242896 | tf_op jit(solution)/shard_map/all_gather | solution.py:85
  230.5 8.7 %fusion.1 = f32[512,640]{1,0:T(8,128)S(1)} fusion(bf16[512,5120]{1,0:T(8,128)(2,1)} %all-gather.7.cloned.1.call-done, bf16[2,5120,640]{2,1,0:T(8,128)(2,1)} %all-gather.9.cloned.1.call-done), kind=kOutput, calls=%fused_computation.5 | convolution fusion | flops 3355443200 | bytes 13107200 | tf_op jit(solution)/shard_map/dot_general | solution.py:118
  239.2 1.2 convolution_add_fusion.3
  240.5 4.3 %fusion = f32[512,640]{1,0:T(8,128)S(1)} fusion(bf16[512,5120]{1,0:T(8,128)(2,1)S(1)} %copy-done.24, bf16[2,5120,640]{2,1,0:T(8,128)(2,1)S(1)} %copy-done.23), kind=kOutput, calls=%fused_computation.3 | convolution fusion | flops 3355443200 | bytes 13107200 | tf_op jit(solution)/shard_map/dot_general | solution.py:125
  244.8 0.5 fusion.9
  245.3 0.4 copy-done.7
  245.7 0.3 convolution_convert_fusion.3
  246.0 27.8 %all-gather.11.cloned.1.call-done = bf16[5120,640]{1,0:T(8,128)(2,1)} async-done(((bf16[640,640]{1,0:T(8,128)(2,1)}), bf16[5120,640]{1,0:T(8,128)(2,1)}) %all-gather.11.cloned.1.call-update) | async-done | bytes 6553616 | tf_op jit(solution)/shard_map/all_gather | solution.py:187
  273.9 7.3 %convolution_convert_fusion.1 = bf16[512,5120]{1,0:T(8,128)(2,1)S(1)} fusion(bf16[512,640]{1,0:T(8,128)(2,1)S(1)} %fusion.9, bf16[5120,640]{1,0:T(8,128)(2,1)} %all-gather.11.cloned.1.call-done), kind=kOutput, calls=%fused_computation.1 | convolution fusion | flops 3358064640 | bytes 12451840 | tf_op jit(solution)/shard_map/dot_general | solution.py:133
  281.2 2.7 pad_maximum_fusion.1
  283.9 0.6 copy-done.22
  284.6 79.0 %reduce-scatter.5.cloned.1.call-done = bf16[32,5248]{1,0:T(8,128)(2,1)} async-done(((bf16[512,5248]{1,0:T(8,128)(2,1)}), bf16[32,5248]{1,0:T(8,128)(2,1)}) %reduce-scatter.5.cloned.1.call-update) | async-done | bytes 335888 | tf_op jit(solution)/shard_map/reduce_scatter | solution.py:91
  363.5 1.0 convert_element_type.125
  364.5 2.4 fusion.6
  (87 shorter events, 1.6 us)
Async XLA Ops:
  7.4 80.9 %copy-start = (bf16[256,5120]{1,0:T(8,128)(2,1)S(1)}, bf16[256,5120]{1,0:T(8,128)(2,1)}, u32[]{:S(2)}) copy-start(bf16[256,5120]{1,0:T(8,128)(2,1)} %param.27) | copy-start | bytes 7864324
  7.4 62.8 %all-gather.5.cloned.1.call-start = ((), (), s32[]{:S(2)}) async-start(), calls=%async_computation.2 | async-start | bytes 5570560 | tf_op jit(solution)/shard_map/all_gather | solution.py:85
  10.6 161.2 %reduce-scatter.3.cloned.1.call-start = ((), (), s32[]{:S(2)}) async-start(), calls=%async_computation.3 | async-start | bytes 5709824 | tf_op jit(solution)/shard_map/reduce_scatter | solution.py:91
  11.8 31.6 %copy-start.15 = (s32[128]{0:T(128)}, s32[128]{0:T(128)S(1)}, u32[]{:S(2)}) copy-start(s32[128]{0:T(128)S(1)} %and_select_fusion) | copy-start | bytes 1540
  11.8 0.5 copy-start.21
  11.9 31.5 %copy-start.17 = (s32[32]{0:T(128)}, s32[32]{0:T(128)S(1)}, u32[]{:S(2)}) copy-start(s32[32]{0:T(128)S(1)} %broadcast_select_fusion) | copy-start | bytes 388
  40.3 3.1 copy-start.19
  40.4 3.0 copy-start.13
  43.4 31.3 %copy-start.11 = (bf16[2,128,64]{1,2,0:T(8,128)(2,1)S(1)}, bf16[2,128,64]{1,2,0:T(8,128)(2,1)}, u32[]{:S(2)}) copy-start(bf16[2,128,64]{1,2,0:T(8,128)(2,1)} %param.30) | copy-start | bytes 98308
  70.2 4.7 %copy-start.2 = (bf16[512,5120]{1,0:T(8,128)(2,1)S(1)}, bf16[512,5120]{1,0:T(8,128)(2,1)}, u32[]{:S(2)}) copy-start(bf16[512,5120]{1,0:T(8,128)(2,1)} %all-gather.5.cloned.1.call-done) | copy-start | bytes 15728644
  70.2 4.7 %copy-start.5 = (bf16[5120,64]{0,1:T(8,128)(2,1)S(1)}, bf16[5120,64]{0,1:T(8,128)(2,1)}, u32[]{:S(2)}) copy-start(bf16[5120,64]{0,1:T(8,128)(2,1)} %param.25) | copy-start | bytes 1966084
  74.9 4.0 %copy-start.25 = (bf16[5120,256]{1,0:T(8,128)(2,1)S(1)}, bf16[5120,256]{1,0:T(8,128)(2,1)}, u32[]{:S(2)}) copy-start(bf16[5120,256]{1,0:T(8,128)(2,1)} %param.24) | copy-start | bytes 7864324
  77.5 3.0 copy-start.9
  77.5 8.6 %collective-permute-start = (bf16[2,512,64]{1,2,0:T(8,128)(2,1)}, bf16[2,512,64]{1,2,0:T(8,128)(2,1)S(1)}, u32[]{:S(2)}, u32[]{:S(2)}) collective-permute-start(bf16[2,512,64]{1,2,0:T(8,128)(2,1)} %maximum_convert_fusion), channel_id=1, source_target_pairs={{0,1},{1,0},{2,3},{3,2},{4,5},{5,4},{6,7},{7,6},{8,9},{9,8},{10,11... | collective-permute-start | bytes 393224 | tf_op jit(solution)/shard_map/ppermute | solution.py:15
  84.7 1.5 copy-start.14
  84.7 1.5 copy-start.20
  84.7 2.1 copy-start.6
  88.3 1.6 copy-start.10
  92.8 79.9 %copy-start.3 = (bf16[1,32,1,5120]{3,1,2,0:T(8,128)(2,1)S(1)}, bf16[1,32,1,5120]{3,1,2,0:T(8,128)(2,1)}, u32[]{:S(2)}) copy-start(bf16[1,32,1,5120]{3,1,2,0:T(8,128)(2,1)} %param.20) | copy-start | bytes 983044
  92.8 79.9 %copy-start.4 = (bf16[128,5120]{1,0:T(8,128)(2,1)S(1)}, bf16[128,5120]{1,0:T(8,128)(2,1)}, u32[]{:S(2)}) copy-start(bf16[128,5120]{1,0:T(8,128)(2,1)} %param.32) | copy-start | bytes 3932164
  92.9 79.9 %copy-start.16 = (s32[128]{0:T(128)S(1)}, s32[128]{0:T(128)}, u32[]{:S(2)}) copy-start(s32[128]{0:T(128)} %copy-done.15) | copy-start | bytes 1540
  92.9 79.9 %copy-start.18 = (s32[32]{0:T(128)S(1)}, s32[32]{0:T(128)}, u32[]{:S(2)}) copy-start(s32[32]{0:T(128)} %copy-done.17) | copy-start | bytes 388
  92.9 80.4 %copy-start.12 = (f32[5120]{0:T(1024)S(1)}, f32[5120]{0:T(1024)}, u32[]{:S(2)}) copy-start(f32[5120]{0:T(1024)} %param.33) | copy-start | bytes 61444
  92.9 107.8 %all-gather.9.cloned.1.call-start = ((), (), s32[]{:S(2)}) async-start(), calls=%async_computation.5 | async-start | bytes 14745600 | tf_op jit(solution)/shard_map/all_gather | solution.py:186
  93.5 137.0 %all-gather.7.cloned.1.call-start = ((), (), s32[]{:S(2)}) async-start(), calls=%async_computation.4 | async-start | bytes 5570560 | tf_op jit(solution)/shard_map/all_gather | solution.py:85
  174.2 99.7 %all-gather.11.cloned.1.call-start = ((), (), s32[]{:S(2)}) async-start(), calls=%async_computation.6 | async-start | bytes 7372800 | tf_op jit(solution)/shard_map/all_gather | solution.py:187
  174.7 188.8 %reduce-scatter.5.cloned.1.call-start = ((), (), s32[]{:S(2)}) async-start(), calls=%async_computation.7 | async-start | bytes 5709824 | tf_op jit(solution)/shard_map/reduce_scatter | solution.py:91
  230.5 10.0 %copy-start.23 = (bf16[2,5120,640]{2,1,0:T(8,128)(2,1)S(1)}, bf16[2,5120,640]{2,1,0:T(8,128)(2,1)}, u32[]{:S(2)}) copy-start(bf16[2,5120,640]{2,1,0:T(8,128)(2,1)} %all-gather.9.cloned.1.call-done) | copy-start | bytes 39321604
  230.5 10.0 %copy-start.24 = (bf16[512,5120]{1,0:T(8,128)(2,1)S(1)}, bf16[512,5120]{1,0:T(8,128)(2,1)}, u32[]{:S(2)}) copy-start(bf16[512,5120]{1,0:T(8,128)(2,1)} %all-gather.7.cloned.1.call-done) | copy-start | bytes 15728644
  240.5 4.3 %copy-start.8 = (bf16[2,128,640]{2,1,0:T(8,128)(2,1)S(1)}, bf16[2,128,640]{2,1,0:T(8,128)(2,1)}, u32[]{:S(2)}) copy-start(bf16[2,128,640]{2,1,0:T(8,128)(2,1)} %param.37) | copy-start | bytes 983044
  244.8 0.9 copy-start.7
  283.9 0.6 copy-start.22
  284.5 82.4 %copy-start.1 = (bf16[256,5120]{1,0:T(8,128)(2,1)S(1)}, bf16[256,5120]{1,0:T(8,128)(2,1)}, u32[]{:S(2)}) copy-start(bf16[256,5120]{1,0:T(8,128)(2,1)} %param.27) | copy-start | bytes 7864324
Sparse Core Ops, SparseCore 0:
  10.7 59.4 all-gather.4
  93.0 78.7 reduce-scatter.2
  284.1 79.3 reduce-scatter.4
Sparse Core Ops, SparseCore 1:
  95.1 69.0 all-gather.8
  174.2 56.2 all-gather.6
  232.0 41.8 all-gather.10
where the time goes:
time: 375 us; the launch traced here: 374 us
  waiting for transfers between devices  243 us (65%)
  blocking collectives  48.4 us (13%)
  matrix products  41.9 us (11%)
  other arithmetic  17.8 us (5%)
  between operations  15.3 us (4%)
  local copies, waits for them, and re-layouts  6.46 us (2%)
    reduce_scatter x2, waiting for transfers between devices, sum_rows(): lax.psum_scatter(term_fn(jnp.int32(0), lax.axis_size('mp') * row_count).a...  157 us
    all_gather x2, waiting for transfers between devices, spread_rows(): lax.all_gather(first_part, 'mp', axis=0, tiled=True)  56.6 us
    all_gather x2, blocking collectives, spread_rows(): lax.all_gather(second_part, 'mp', axis=0, tiled=True)  48.4 us
    all_gather x1, waiting for transfers between devices, shards(): lax.all_gather(down_weight, 'req', axis=0, tiled=True)  27.8 us
    dot_general x1, matrix products, feed_forward(): jnp.dot(mlp_all, gate_up_full[0], preferred_element_type=jnp.float32)  8.72 us
  transfers between devices with their start and end apart: 7, of which 5 were waited for; matrix products, arithmetic and copies ran while one was open for 9% of the time, Pallas kernels for 0%

commit v1 on v0

--- a/solution.py
+++ b/solution.py
@@ -184,7 +184,9 @@
     total_rows = slot_dev * mp_count
     gate_up_full, down_full = (
         lax.all_gather(gate_up_weight, "req", axis=1, tiled=True),
-        lax.all_gather(down_weight, "req", axis=0, tiled=True),
+        jnp.concatenate(
+            lax.all_to_all(jnp.stack([down_weight] * lax.axis_size("req")), "req", 0, 0), axis=0
+        ),
     )
     local_rows = states.reshape(slot_dev, model_width)
     own_lengths = lax.dynamic_index_in_dim(lengths, group_index, 0, keepdims=False)

time: 375 us -> 356 us (0.949)
  waiting for transfers between devices: 243 us -> 216 us
  starting transfers between devices: 1.82 us -> 6.68 us
    all_gather x1 -> x0, waiting for transfers between devices: 27.8 us -> none  [shards(): lax.all_gather(down_weight, 'req', axis=0, tiled=True)]
    all_to_all x0 -> x1, waiting for transfers between devices: none -> 12.9 us  [shards(): lax.all_to_all(jnp.stack([down_weight] * lax.axis_size('req')), 'req', 0, 0)]
    all_gather x2, waiting for transfers between devices: 56.6 us -> 48.4 us  [spread_rows(): lax.all_gather(first_part, 'mp', axis=0, tiled=True)]
    all_to_all x0 -> x1, starting transfers between devices: none -> 4.9 us  [shards(): lax.all_to_all(jnp.stack([down_weight] * lax.axis_size('req')), 'req', 0, 0)]
  transfers between devices with their start and end apart: 7 -> 7, of which waited for: 5 -> 5; matrix products, arithmetic and copies ran while one was open for 9% -> 10% of each run, Pallas kernels for 0% -> 0%
where the time goes in v1:
time: 356 us; the launch traced here: 355 us
  waiting for transfers between devices  216 us (61%)
  blocking collectives  48.2 us (14%)
  matrix products  41.9 us (12%)
  other arithmetic  17.9 us (5%)
  between operations  15.1 us (4%)
  local copies, waits for them, and re-layouts  9.47 us (3%)
  starting transfers between devices  6.68 us (2%)
    reduce_scatter x2, waiting for transfers between devices, sum_rows(): lax.psum_scatter(term_fn(jnp.int32(0), lax.axis_size('mp') * row_count).a...  154 us
    all_gather x2, waiting for transfers between devices, spread_rows(): lax.all_gather(first_part, 'mp', axis=0, tiled=True)  48.4 us
    all_gather x2, blocking collectives, spread_rows(): lax.all_gather(second_part, 'mp', axis=0, tiled=True)  48.2 us
    all_to_all x1, waiting for transfers between devices, shards(): lax.all_to_all(jnp.stack([down_weight] * lax.axis_size('req')), 'req', 0, 0)  12.9 us
    dot_general x1, matrix products, feed_forward(): jnp.dot(mlp_all, gate_up_full[0], preferred_element_type=jnp.float32)  8.58 us
    dot_general x1, matrix products, down_term(): lax.dot_general(hidden_activation, down_full, (((1,), (1,)), ((), ())), p...  7.39 us
  transfers between devices with their start and end apart: 7, of which 5 were waited for; matrix products, arithmetic and copies ran while one was open for 10% of the time, Pallas kernels for 0%

profile of v1, /device:TPU:0, one launch (start us, length us, event | category | flops | bytes accessed | tf_op | source)
XLA Modules:
  0.0 355.2 jit_solution(3544653466798567951)
XLA Ops:
  7.4 1.3 fusion.17
  8.7 1.9 fusion.19
  10.6 0.9 dynamic-slice_reduce_fusion
  12.0 0.4 copy-done.23
  12.4 2.9 fusion.12
  15.3 25.0 %all_gather.16 = bf16[512,384]{1,0:T(8,128)(2,1)S(1)} all-gather(bf16[32,384]{1,0:T(8,128)(2,1)S(1)} %fusion.12), channel_id=1, replica_groups=mesh['req'=8,'mp'=16] {'mp'}, dimensions={0}, use_global_device_ids=true | all-gather | bytes 417792 | tf_op jit(solution)/shard_map/all_gather | solution.py:86
  40.5 1.2 fusion.16
  41.6 1.9 multiply_cosine_fusion
  43.5 26.7 %all-gather.4.cloned.1.call-done = bf16[512,5120]{1,0:T(8,128)(2,1)} async-done(((bf16[32,5120]{1,0:T(8,128)(2,1)}), bf16[512,5120]{1,0:T(8,128)(2,1)}) %all-gather.4.cloned.1.call-update) | async-done | bytes 5242896 | tf_op jit(solution)/shard_map/all_gather | solution.py:85
  70.2 4.5 %fusion.76 = f32[512,64]{0,1:T(8,128)S(1)} fusion(bf16[512,5120]{1,0:T(8,128)(2,1)} %all-gather.4.cloned.1.call-done, bf16[5120,64]{0,1:T(8,128)(2,1)} %param.26), kind=kOutput, calls=%fused_computation.140 | convolution fusion | flops 335544320 | bytes 6029312 | tf_op jit(solution)/shard_map/dot_general | solution.py:227
  74.9 1.7 fusion.75
  76.8 0.7 maximum_convert_fusion
  77.5 1.4 collective-permute-start
  78.9 1.6 fusion.77
  80.5 0.3 convolution_add_fusion.4
  80.8 0.8 fusion.73
  81.6 1.1 copy.44
  82.8 2.0 copy.45
  84.7 1.4 subtract_convert_fusion
  86.2 0.6 fusion.45
  86.8 0.6 fusion.74
  87.4 0.3 fusion.7
  87.7 0.5 convolution_convert_fusion.2
  88.3 1.6 convolution_convert_fusion
  89.9 0.3 convolution_convert_fusion.4
  90.1 2.7 pad_maximum_fusion
  92.9 0.5 all-gather.8.cloned.1.call-update
  93.7 78.0 %reduce-scatter.3.cloned.1.call-done = bf16[32,5248]{1,0:T(8,128)(2,1)} async-done(((bf16[512,5248]{1,0:T(8,128)(2,1)}), bf16[32,5248]{1,0:T(8,128)(2,1)}) %reduce-scatter.3.cloned.1.call-update) | async-done | bytes 335888 | tf_op jit(solution)/shard_map/reduce_scatter | solution.py:91
  171.7 1.0 convert_element_type.118
  172.8 0.5 multiply_reduce_fusion
  173.3 0.9 multiply_convert_fusion
  174.2 3.3 stack.11
  177.4 4.9 %all-to-all-start = ((bf16[8,640,640]{2,1,0:T(8,128)(2,1)}), bf16[8,640,640]{2,1,0:T(8,128)(2,1)}, u32[]{:S(2)}, u32[]{:S(2)}) async-start(bf16[8,640,640]{2,1,0:T(8,128)(2,1)} %stack.11), calls=%async_computation.1 | async-start | bytes 13107200 | tf_op jit(solution)/shard_map/all_to_all | solution.py:188
  182.4 2.4 fusion.13
  184.9 23.1 %all_gather.19 = bf16[512,256]{1,0:T(8,128)(2,1)S(1)} all-gather(bf16[32,256]{1,0:T(8,128)(2,1)S(1)} %fusion.13), channel_id=1, replica_groups=mesh['req'=8,'mp'=16] {'mp'}, dimensions={0}, use_global_device_ids=true | all-gather | bytes 278528 | tf_op jit(solution)/shard_map/all_gather | solution.py:86
  208.1 21.7 %all-gather.6.cloned.1.call-done = bf16[512,5120]{1,0:T(8,128)(2,1)} async-done(((bf16[32,5120]{1,0:T(8,128)(2,1)}), bf16[512,5120]{1,0:T(8,128)(2,1)}) %all-gather.6.cloned.1.call-update) | async-done | bytes 5242896 | tf_op jit(solution)/shard_map/all_gather | solution.py:85
  229.8 8.6 %fusion.1 = f32[512,640]{1,0:T(8,128)S(1)} fusion(bf16[512,5120]{1,0:T(8,128)(2,1)} %all-gather.6.cloned.1.call-done, bf16[2,5120,640]{2,1,0:T(8,128)(2,1)} %all-gather.8.cloned.1.call-done), kind=kOutput, calls=%fused_computation.5 | convolution fusion | flops 3355443200 | bytes 13107200 | tf_op jit(solution)/shard_map/dot_general | solution.py:118
  238.3 1.3 convolution_add_fusion.3
  239.6 4.3 %fusion = f32[512,640]{1,0:T(8,128)S(1)} fusion(bf16[512,5120]{1,0:T(8,128)(2,1)S(1)} %copy-done.26, bf16[2,5120,640]{2,1,0:T(8,128)(2,1)S(1)} %copy-done.25), kind=kOutput, calls=%fused_computation.3 | convolution fusion | flops 3355443200 | bytes 13107200 | tf_op jit(solution)/shard_map/dot_general | solution.py:125
  243.9 0.5 fusion.9
  244.4 12.9 %all-to-all-done = bf16[8,640,640]{2,1,0:T(8,128)(2,1)} async-done(((bf16[8,640,640]{2,1,0:T(8,128)(2,1)}), bf16[8,640,640]{2,1,0:T(8,128)(2,1)}, u32[]{:S(2)}, u32[]{:S(2)}) %all-to-all-start) | async-done | bytes 6553632 | tf_op jit(solution)/shard_map/all_to_all | solution.py:188
  257.3 7.4 %convolution_convert_fusion.1 = bf16[512,5120]{1,0:T(8,128)(2,1)S(1)} fusion(bf16[512,640]{1,0:T(8,128)(2,1)S(1)} %fusion.9, bf16[5120,640]{1,0:T(8,128)(2,1)} %bitcast.25), kind=kOutput, calls=%fused_computation.1 | convolution fusion | flops 3358064640 | bytes 12451840 | tf_op jit(solution)/shard_map/dot_general | solution.py:133
  264.7 0.3 convolution_convert_fusion.3
  265.1 2.7 pad_maximum_fusion.1
  267.8 0.6 copy-done.24
  268.5 76.2 %reduce-scatter.5.cloned.1.call-done = bf16[32,5248]{1,0:T(8,128)(2,1)} async-done(((bf16[512,5248]{1,0:T(8,128)(2,1)}), bf16[32,5248]{1,0:T(8,128)(2,1)}) %reduce-scatter.5.cloned.1.call-update) | async-done | bytes 335888 | tf_op jit(solution)/shard_map/reduce_scatter | solution.py:91
  344.7 1.0 convert_element_type.125
  345.7 2.4 fusion.6
  (91 shorter events, 1.6 us)
Async XLA Ops:
  7.4 80.9 %copy-start = (bf16[256,5120]{1,0:T(8,128)(2,1)S(1)}, bf16[256,5120]{1,0:T(8,128)(2,1)}, u32[]{:S(2)}) copy-start(bf16[256,5120]{1,0:T(8,128)(2,1)} %param.27) | copy-start | bytes 7864324
  7.4 62.8 %all-gather.4.cloned.1.call-start = ((), (), s32[]{:S(2)}) async-start(), calls=%async_computation.3 | async-start | bytes 5570560 | tf_op jit(solution)/shard_map/all_gather | solution.py:85
  10.6 161.2 %reduce-scatter.3.cloned.1.call-start = ((), (), s32[]{:S(2)}) async-start(), calls=%async_computation.4 | async-start | bytes 5709824 | tf_op jit(solution)/shard_map/reduce_scatter | solution.py:91
  11.8 31.7 %copy-start.17 = (s32[128]{0:T(128)}, s32[128]{0:T(128)S(1)}, u32[]{:S(2)}) copy-start(s32[128]{0:T(128)S(1)} %and_select_fusion) | copy-start | bytes 1540
  11.8 0.6 copy-start.23
  11.9 31.6 %copy-start.19 = (s32[32]{0:T(128)}, s32[32]{0:T(128)S(1)}, u32[]{:S(2)}) copy-start(s32[32]{0:T(128)S(1)} %broadcast_select_fusion) | copy-start | bytes 388
  15.3 59.4 %copy-start.13 = (bf16[2,128,64]{1,2,0:T(8,128)(2,1)S(1)}, bf16[2,128,64]{1,2,0:T(8,128)(2,1)}, u32[]{:S(2)}) copy-start(bf16[2,128,64]{1,2,0:T(8,128)(2,1)} %param.30) | copy-start | bytes 98308
  40.3 3.2 copy-start.21
  40.5 3.0 copy-start.15
  70.2 4.7 %copy-start.2 = (bf16[512,5120]{1,0:T(8,128)(2,1)S(1)}, bf16[512,5120]{1,0:T(8,128)(2,1)}, u32[]{:S(2)}) copy-start(bf16[512,5120]{1,0:T(8,128)(2,1)} %all-gather.4.cloned.1.call-done) | copy-start | bytes 15728644
  70.2 4.7 %copy-start.7 = (bf16[5120,64]{0,1:T(8,128)(2,1)S(1)}, bf16[5120,64]{0,1:T(8,128)(2,1)}, u32[]{:S(2)}) copy-start(bf16[5120,64]{0,1:T(8,128)(2,1)} %param.25) | copy-start | bytes 1966084
  74.7 4.2 %copy-start.27 = (bf16[5120,256]{1,0:T(8,128)(2,1)S(1)}, bf16[5120,256]{1,0:T(8,128)(2,1)}, u32[]{:S(2)}) copy-start(bf16[5120,256]{1,0:T(8,128)(2,1)} %param.24) | copy-start | bytes 7864324
  77.5 3.0 copy-start.11
  77.5 8.6 %collective-permute-start = (bf16[2,512,64]{1,2,0:T(8,128)(2,1)}, bf16[2,512,64]{1,2,0:T(8,128)(2,1)S(1)}, u32[]{:S(2)}, u32[]{:S(2)}) collective-permute-start(bf16[2,512,64]{1,2,0:T(8,128)(2,1)} %maximum_convert_fusion), channel_id=1, source_target_pairs={{0,1},{1,0},{2,3},{3,2},{4,5},{5,4},{6,7},{7,6},{8,9},{9,8},{10,11... | collective-permute-start | bytes 393224 | tf_op jit(solution)/shard_map/ppermute | solution.py:15
  84.7 1.5 copy-start.16
  84.7 1.5 copy-start.22
  84.7 2.1 copy-start.8
  88.3 1.6 copy-start.12
  92.8 79.9 %copy-start.4 = (bf16[1,32,1,5120]{3,1,2,0:T(8,128)(2,1)S(1)}, bf16[1,32,1,5120]{3,1,2,0:T(8,128)(2,1)}, u32[]{:S(2)}) copy-start(bf16[1,32,1,5120]{3,1,2,0:T(8,128)(2,1)} %param.20) | copy-start | bytes 983044
  92.8 79.9 %copy-start.5 = (bf16[128,5120]{1,0:T(8,128)(2,1)S(1)}, bf16[128,5120]{1,0:T(8,128)(2,1)}, u32[]{:S(2)}) copy-start(bf16[128,5120]{1,0:T(8,128)(2,1)} %param.32) | copy-start | bytes 3932164
  92.8 79.9 %copy-start.18 = (s32[128]{0:T(128)S(1)}, s32[128]{0:T(128)}, u32[]{:S(2)}) copy-start(s32[128]{0:T(128)} %copy-done.17) | copy-start | bytes 1540
  92.8 79.9 %copy-start.20 = (s32[32]{0:T(128)S(1)}, s32[32]{0:T(128)}, u32[]{:S(2)}) copy-start(s32[32]{0:T(128)} %copy-done.19) | copy-start | bytes 388
  92.8 80.4 %copy-start.14 = (f32[5120]{0:T(1024)S(1)}, f32[5120]{0:T(1024)}, u32[]{:S(2)}) copy-start(f32[5120]{0:T(1024)} %param.33) | copy-start | bytes 61444
  92.9 81.3 %copy-start.6 = (bf16[640,640]{1,0:T(8,128)(2,1)S(1)}, bf16[640,640]{1,0:T(8,128)(2,1)}, u32[]{:S(2)}) copy-start(bf16[640,640]{1,0:T(8,128)(2,1)} %param.35) | copy-start | bytes 2457604
  92.9 115.2 %all-gather.8.cloned.1.call-start = ((), (), s32[]{:S(2)}) async-start(), calls=%async_computation.6 | async-start | bytes 14745600 | tf_op jit(solution)/shard_map/all_gather | solution.py:186
  93.5 136.3 %all-gather.6.cloned.1.call-start = ((), (), s32[]{:S(2)}) async-start(), calls=%async_computation.5 | async-start | bytes 5570560 | tf_op jit(solution)/shard_map/all_gather | solution.py:85
  177.4 5.0 %copy-start.3 = (bf16[32,5120]{1,0:T(8,128)(2,1)S(1)}, bf16[32,5120]{1,0:T(8,128)(2,1)}, u32[]{:S(2)}) copy-start(bf16[32,5120]{1,0:T(8,128)(2,1)} %multiply_convert_fusion) | copy-start | bytes 983044
  177.4 79.9 %all-to-all-start = ((bf16[8,640,640]{2,1,0:T(8,128)(2,1)}), bf16[8,640,640]{2,1,0:T(8,128)(2,1)}, u32[]{:S(2)}, u32[]{:S(2)}) async-start(bf16[8,640,640]{2,1,0:T(8,128)(2,1)} %stack.11), calls=%async_computation.1 | async-start | bytes 13107200 | tf_op jit(solution)/shard_map/all_to_all | solution.py:188
  182.4 162.3 %reduce-scatter.5.cloned.1.call-start = ((), (), s32[]{:S(2)}) async-start(), calls=%async_computation.7 | async-start | bytes 5709824 | tf_op jit(solution)/shard_map/reduce_scatter | solution.py:91
  229.7 9.9 %copy-start.25 = (bf16[2,5120,640]{2,1,0:T(8,128)(2,1)S(1)}, bf16[2,5120,640]{2,1,0:T(8,128)(2,1)}, u32[]{:S(2)}) copy-start(bf16[2,5120,640]{2,1,0:T(8,128)(2,1)} %all-gather.8.cloned.1.call-done) | copy-start | bytes 39321604
  229.7 9.9 %copy-start.26 = (bf16[512,5120]{1,0:T(8,128)(2,1)S(1)}, bf16[512,5120]{1,0:T(8,128)(2,1)}, u32[]{:S(2)}) copy-start(bf16[512,5120]{1,0:T(8,128)(2,1)} %all-gather.6.cloned.1.call-done) | copy-start | bytes 15728644
  239.6 4.3 %copy-start.10 = (bf16[2,128,640]{2,1,0:T(8,128)(2,1)S(1)}, bf16[2,128,640]{2,1,0:T(8,128)(2,1)}, u32[]{:S(2)}) copy-start(bf16[2,128,640]{2,1,0:T(8,128)(2,1)} %param.37) | copy-start | bytes 983044
  257.3 7.4 %copy-start.9 = (bf16[640,128]{1,0:T(8,128)(2,1)S(1)}, bf16[640,128]{1,0:T(8,128)(2,1)}, u32[]{:S(2)}) copy-start(bf16[640,128]{1,0:T(8,128)(2,1)} %param.38) | copy-start | bytes 491524
  267.8 0.7 copy-start.24
  267.8 80.3 %copy-start.1 = (bf16[256,5120]{1,0:T(8,128)(2,1)S(1)}, bf16[256,5120]{1,0:T(8,128)(2,1)}, u32[]{:S(2)}) copy-start(bf16[256,5120]{1,0:T(8,128)(2,1)} %param.27) | copy-start | bytes 7864324
Sparse Core Ops, SparseCore 0:
  10.7 59.4 all-gather.3
  93.0 78.6 reduce-scatter.2
  267.9 76.6 reduce-scatter.4
Sparse Core Ops, SparseCore 1:
  95.1 69.0 all-gather.7
  174.2 55.5 all-gather.5
